TPU v7x, 512 devices: a whole 4x4x16 slice. The times are simulated.
512 devices in a mesh: ingest: 8 (over y, core), owner: 64 (over x, z).
Axes of the slice: x: 4, y: 4, z: 16, core: 2. Of those that a mesh axis runs over, the one named last changes fastest.
Arguments:
- frame_rows: bfloat16 [2112, 28, 1024], P('owner', None, 'ingest'), may hold values from -32 to 32
- route_owner: int32 [2112], P('owner'), may hold values from 0 to 63, as said below
- route_slot: int32 [2112], P('owner'), may hold values from 0 to 32, as said below
- frames: int32 [2112], P('owner'), may hold values from 1 to 28, as said below
- kv_cache: bfloat16 [2112, 8, 70, 256], P('owner', 'ingest'), may hold values from -250 to 250
- conv_cache: bfloat16 [2112, 8, 1024], P('owner', None, 'ingest'), may hold values from -5 to 5
- mig_owner: int32 [2048], P('owner'), may hold values from 0 to 63, as said below
- ln1_gain: float32 [1024], replicated, may hold values from 0.1 to 1.9
- w_qkv: bfloat16 [1024, 8, 384], P(None, 'ingest'), may hold values from -0.1875 to 0.1875
- w_out: bfloat16 [1024, 1024], P('ingest'), may hold values from -0.1875 to 0.1875
- ln2_gain: float32 [1024], replicated, may hold values from 0.1 to 1.9
- w_pw1: bfloat16 [1024, 2, 1024], P(None, None, 'ingest'), may hold values from -0.1875 to 0.1875
- dw_weight: bfloat16 [9, 1024], P(None, 'ingest'), may hold values from -2 to 2
- bn_scale: float32 [1024], P('ingest'), may hold values from 0.1 to 1.9
- bn_shift: float32 [1024], P('ingest'), may hold values from -2.5 to 2.5
- w_pw2: bfloat16 [1024, 1024], P('ingest'), may hold values from -0.1875 to 0.1875
Outputs:
- layer_out: bfloat16 [2112, 28, 1024], P('owner', None, 'ingest')
- kv_next: bfloat16 [2112, 8, 70, 256], P('owner', 'ingest')
- conv_next: bfloat16 [2112, 8, 1024], P('owner', None, 'ingest')
Inputs may be any that keep to these rules, and one draw needn't show every extreme that they name: `route_owner`: every owner receives exactly 33 utterances. The utterances that one source device along owner (a block of 33 rows in arrival order) sends to one owner number at most 1, and some source device reaches that number. `route_slot`: the utterances sent to one owner have distinct slots. Every owner holds an utterance with 28 new frames. The utterance in old slot 1 + j of an owner moves to slot 1 + j of owner mig_owner; the 32 utterances of one owner go to 32 different other owners, and every owner receives exactly one utterance for each j.
All inputs are finite; a program needn't handle non-finite values.
Results may differ from a plain program's by a relative error of at most 0.01.
Values may be sent and summed in bfloat16 or wider, within the bound.
No kernel may reach another device: no remote copies, remote signals or barrier semaphores. Data moves between devices by JAX's collectives and lax.ppermute only.
A program may use at most 64 MiB of HBM per device.

v0:
```python
import jax
import jax.numpy as jnp
from jax import lax
from jax.sharding import PartitionSpec as P

BLOCKS = 2
norm_eps = 1e-05


def normalize(values, gain_cols):
    model_width = values.shape[-1]
    row_mean = jnp.sum(values, axis=-1, keepdims=True) / model_width
    spread = jnp.sum(values * values, axis=-1, keepdims=True) / model_width - row_mean * row_mean
    return ((values - row_mean) * lax.rsqrt(spread + norm_eps) * gain_cols).astype(jnp.bfloat16)


def one_hot_rows(table, rows):
    return jnp.dot(table.astype(jnp.bfloat16), rows, preferred_element_type=jnp.float32).astype(
        jnp.bfloat16
    )


def grouped_terms(left_groups, right_groups):
    terms = jnp.einsum(
        "grc,gcn->grn", left_groups, right_groups, preferred_element_type=jnp.float32
    ).astype(jnp.bfloat16)
    return jnp.sum(terms.astype(jnp.float32), axis=0)


def shards(
    frame_rows,
    route_owner,
    route_slot,
    frames,
    kv_cache,
    conv_cache,
    mig_owner,
    ln1_gain,
    w_qkv,
    w_out,
    ln2_gain,
    w_pw1,
    dw_weight,
    bn_scale,
    bn_shift,
    w_pw2,
):
    owners = lax.axis_size("owner")
    groups = lax.axis_size("ingest")
    me = lax.axis_index("ingest")
    utterances, frame_span, local_width = frame_rows.shape
    model_width = w_qkv.shape[0]
    head_dim = w_qkv.shape[2] // 3
    cache_len = kv_cache.shape[2]
    conv_len = conv_cache.shape[1]
    taps = dw_weight.shape[0]
    horizon = frame_span // BLOCKS
    moving = mig_owner.shape[0]
    settled = utterances - moving
    lanes = 128
    w_out_full = lax.all_gather(w_out, "ingest", axis=0, tiled=True)
    w_pw2_cols = lax.all_to_all(
        w_pw2.reshape(local_width, groups, local_width).transpose(1, 0, 2),
        "ingest",
        split_axis=0,
        concat_axis=0,
        tiled=True,
    )
    dest = jnp.arange(owners, dtype=jnp.int32)
    frame_flat = frame_rows.reshape(utterances, frame_span * local_width)
    slot_tag = jnp.broadcast_to((route_slot + 1).astype(jnp.bfloat16)[:, None], (utterances, lanes))
    frame_send = one_hot_rows(
        dest[:, None] == route_owner[None, :], jnp.concatenate([frame_flat, slot_tag], axis=1)
    )
    kv_width = cache_len * 2 * head_dim
    conv_width = conv_len * local_width
    mover_tag = jnp.broadcast_to(
        (jnp.arange(moving, dtype=jnp.int32) + 1).astype(jnp.bfloat16)[:, None], (moving, lanes)
    )
    cache_rows = jnp.concatenate(
        [
            kv_cache[settled:].reshape(moving, kv_width),
            conv_cache[settled:].reshape(moving, conv_width),
            mover_tag,
        ],
        axis=1,
    )
    cache_send = one_hot_rows(dest[:, None] == mig_owner[None, :], cache_rows)
    frame_cols = frame_send.shape[1]
    arrived = lax.all_to_all(
        jnp.concatenate([frame_send, cache_send], axis=1),
        "owner",
        split_axis=0,
        concat_axis=0,
        tiled=True,
    )
    frame_part = frame_span * local_width
    got_slot = arrived[:, frame_part].astype(jnp.int32)
    slots = jnp.arange(utterances, dtype=jnp.int32)
    arranged = one_hot_rows(
        slots[:, None] + 1 == got_slot[None, :], arrived[:, :frame_part]
    ).reshape(utterances, frame_span, local_width)
    got_mover = arrived[:, frame_cols + kv_width + conv_width].astype(jnp.int32)
    movers = jnp.arange(moving, dtype=jnp.int32)
    moved = one_hot_rows(
        movers[:, None] + 1 == got_mover[None, :],
        arrived[:, frame_cols : frame_cols + kv_width + conv_width],
    )
    kv_state = jnp.concatenate(
        [
            kv_cache[:settled].reshape(settled, cache_len, 2 * head_dim),
            moved[:, :kv_width].reshape(moving, cache_len, 2 * head_dim),
        ],
        axis=0,
    )
    conv_state = jnp.concatenate(
        [conv_cache[:settled], moved[:, kv_width:].reshape(moving, conv_len, local_width)], axis=0
    )
    x_all = lax.all_gather(arranged, "ingest", axis=0, tiled=False)
    x_rows = x_all.transpose(1, 2, 0, 3).reshape(utterances, frame_span, model_width)
    x_rows = x_rows.astype(jnp.float32)
    normed = normalize(x_rows, ln1_gain)
    projected = jnp.dot(
        normed, w_qkv.reshape(model_width, 3 * head_dim), preferred_element_type=jnp.float32
    )
    queries = projected[..., :head_dim].astype(jnp.bfloat16)
    fresh = projected[..., head_dim:].astype(jnp.bfloat16)
    memory = jnp.concatenate([kv_state, fresh], axis=1)
    keys_total = memory.shape[1]
    scores = jnp.einsum(
        "sqd,skd->sqk", queries, memory[..., :head_dim], preferred_element_type=jnp.float32
    ) * head_dim ** (-0.5)
    frame_index = jnp.arange(frame_span, dtype=jnp.int32)
    block_of = frame_index // horizon
    low = block_of * horizon
    high = cache_len + jnp.minimum(frames[:, None], (block_of[None, :] + 1) * horizon)
    position = jnp.arange(keys_total, dtype=jnp.int32)
    live_keys = (position[None, None, :] >= low[None, :, None]) & (
        position[None, None, :] < high[:, :, None]
    )
    scores = jnp.where(live_keys, scores, -1e30)
    row_max = jnp.max(scores, axis=-1, keepdims=True)
    weights = jnp.exp(scores - row_max)
    probabilities = (weights / jnp.sum(weights, axis=-1, keepdims=True)).astype(jnp.bfloat16)
    context = jnp.einsum(
        "sqk,skd->sqd", probabilities, memory[..., head_dim:], preferred_element_type=jnp.float32
    ).astype(jnp.bfloat16)
    ctx_all = lax.all_gather(context, "ingest", axis=0, tiled=False)
    row_count = utterances * frame_span
    attn = grouped_terms(
        ctx_all.reshape(groups, row_count, head_dim),
        w_out_full.reshape(groups, head_dim, model_width),
    )
    residual = x_rows.reshape(row_count, model_width) + attn
    normed2 = normalize(residual, ln2_gain)
    mixed = jnp.dot(
        normed2, w_pw1.reshape(model_width, 2 * local_width), preferred_element_type=jnp.float32
    )
    glu_out = (mixed[:, :local_width] * jax.nn.sigmoid(mixed[:, local_width:])).astype(jnp.bfloat16)
    glu_out = glu_out.reshape(utterances, frame_span, local_width)
    joined = jnp.concatenate([conv_state, glu_out], axis=1)
    joined_f = joined.astype(jnp.float32)
    running = jnp.zeros((utterances, frame_span, local_width), jnp.float32)
    for tap_index in range(taps):
        running = running + joined_f[:, tap_index : tap_index + frame_span, :] * dw_weight[
            tap_index
        ].astype(jnp.float32)
    activated = jax.nn.silu(running * bn_scale + bn_shift).astype(jnp.bfloat16)
    act_all = lax.all_gather(activated, "ingest", axis=0, tiled=False)
    conv_terms = grouped_terms(act_all.reshape(groups, row_count, local_width), w_pw2_cols)
    residual_own = lax.dynamic_slice_in_dim(residual, me * local_width, local_width, 1)
    result = (residual_own + conv_terms).reshape(utterances, frame_span, local_width)
    live_rows = frame_index[None, :] < frames[:, None]
    layer_out = jnp.where(live_rows[:, :, None], result, 0.0).astype(jnp.bfloat16)
    keep = jnp.arange(cache_len, dtype=jnp.int32)
    kv_pick = position[None, None, :] == keep[None, :, None] + frames[:, None, None]
    kv_next = jnp.einsum(
        "srp,spd->srd", kv_pick.astype(jnp.bfloat16), memory, preferred_element_type=jnp.float32
    ).astype(jnp.bfloat16)
    conv_keep = jnp.arange(conv_len, dtype=jnp.int32)
    conv_pos = jnp.arange(joined.shape[1], dtype=jnp.int32)
    conv_pick = conv_pos[None, None, :] == conv_keep[None, :, None] + frames[:, None, None]
    conv_next = jnp.einsum(
        "srp,spd->srd", conv_pick.astype(jnp.bfloat16), joined, preferred_element_type=jnp.float32
    ).astype(jnp.bfloat16)
    return (layer_out, kv_next.reshape(kv_cache.shape), conv_next)


def solution(mesh):
    in_specs = (
        P("owner", None, "ingest"),
        P("owner"),
        P("owner"),
        P("owner"),
        P("owner", "ingest", None, None),
        P("owner", None, "ingest"),
        P("owner"),
        P(),
        P(None, "ingest", None),
        P("ingest", None),
        P(),
        P(None, None, "ingest"),
        P(None, "ingest"),
        P("ingest"),
        P("ingest"),
        P("ingest", None),
    )
    out_specs = (
        P("owner", None, "ingest"),
        P("owner", "ingest", None, None),
        P("owner", None, "ingest"),
    )
    return jax.shard_map(shards, mesh=mesh, in_specs=in_specs, out_specs=out_specs, check_vma=False)
```

profile of v0, /device:TPU:1, one launch (start us, length us, event | category | flops | bytes accessed | tf_op | source)
XLA Modules:
  0.0 387.9 jit_solution(17638379592714041639)
XLA Ops:
  7.3 1.5 slice-done
  8.8 0.2 copy.37
  9.3 0.3 convolution_convert_fusion.2
  9.7 0.8 convolution_convert_fusion
  10.5 1.8 maximum_bitcast_fusion
  12.3 0.5 broadcast.254
  12.8 5.4 %reduce.8 = bf16[64,22784]{1,0:T(8,128)(2,1)} reduce(bf16[64,1,22784]{2,0,1:T(8,128)(2,1)} %maximum_bitcast_fusion, bf16[]{:T(256)} %broadcast.254), dimensions={1}, to_apply=%copy.30.reduce_sub_computation | reduce | bytes 5832706 | tf_op jit(solution)/shard_map/all_to_all | solution.py:90
  18.2 4.4 %reshape.407 = bf16[64,2,11392]{2,1,0:T(2,128)(2,1)} reshape(bf16[64,22784]{1,0:T(8,128)(2,1)} %reduce.8) | data formatting | bytes 5832704
  22.6 19.3 %all-to-all-start = ((bf16[64,2,11392]{2,1,0:T(2,128)(2,1)}), bf16[64,2,11392]{2,1,0:T(2,128)(2,1)}, u32[]{:S(2)}, u32[]{:S(2)}) async-start(bf16[64,2,11392]{2,1,0:T(2,128)(2,1)} %reshape.407), calls=%async_computation | async-start | bytes 5832704 | tf_op jit(solution)/shard_map/all_to_all | solution.py:90
  42.0 127.4 %all-to-all-done = bf16[64,2,11392]{2,1,0:T(2,128)(2,1)} async-done(((bf16[64,2,11392]{2,1,0:T(2,128)(2,1)}), bf16[64,2,11392]{2,1,0:T(2,128)(2,1)}, u32[]{:S(2)}, u32[]{:S(2)}) %all-to-all-start) | async-done | bytes 2916384 | tf_op jit(solution)/shard_map/all_to_all | solution.py:90
  169.5 16.8 %reshape.408 = bf16[64,1,22784]{2,1,0:T(2,128)(2,1)} reshape(bf16[64,2,11392]{2,1,0:T(2,128)(2,1)} %all-to-all-done) | data formatting | bytes 5832704
  186.2 3.1 copy.57
  189.4 1.5 copy-done.3
  190.9 0.3 convolution_convert_fusion.3
  191.2 0.9 all_gather_reshape.3
  192.1 0.2 all-gather.11.cloned.1.call-start
  192.5 2.2 convolution_convert_fusion.1
  194.7 1.2 slice.143
  195.9 2.5 reshape.378
  198.4 26.5 %all-gather.7.cloned.1.call-done = bf16[8,33,28,128]{3,2,1,0:T(8,128)(2,1)} async-done(((bf16[1,33,28,128]{3,2,1,0:T(8,128)(2,1)}), bf16[8,33,28,128]{3,2,1,0:T(8,128)(2,1)}) %all-gather.7.cloned.1.call-update) | async-done | bytes 1892368 | tf_op jit(solution)/shard_map/all_gather | solution.py:119
  224.9 5.3 %bitcast_reduce_fusion = (f32[33,28]{1,0:T(8,128)S(1)}, f32[33,28]{1,0:T(8,128)S(1)}) fusion(bf16[8,33,28,128]{3,2,1,0:T(8,128)(2,1)} %all-gather.7.cloned.1.call-done), kind=kLoop, calls=%fused_computation.9 | loop fusion | flops 3782856 | bytes 1899744 | tf_op jit(solution)/shard_map/reduce_sum | solution.py:12
  230.3 5.5 %fusion.3 = bf16[33,28,8,128]{3,2,1,0:T(8,128)(2,1)} fusion(f32[8,128]{1,0:T(8,128)S(1)} %bitcast.128, f32[33,28]{1,0:T(8,128)S(1)} %get-tuple-element.24, f32[33,28]{1,0:T(8,128)S(1)} %get-tuple-element.23, bf16[8,33,28,128]{3,2,1,0:T(8,128)(2,1)S(1)} %copy-done.2), kind=kLoop, calls=%fused_computation.13 | loop fusion | flops 4730880 | bytes 3796192 | tf_op jit(solution)/shard_map/convert_element_type | solution.py:14
  235.7 4.1 %convert_element_type.219 = bf16[33,28,1024]{2,1,0:T(8,128)(2,1)} reshape(bf16[33,28,8,128]{3,2,1,0:T(8,128)(2,1)} %fusion.3) | data formatting | bytes 3784704 | tf_op jit(solution)/shard_map/convert_element_type | solution.py:14
  239.9 3.0 convolution_convert_fusion.5
  242.9 0.3 pad_maximum_fusion
  243.3 1.2 copy-done.9
  244.5 0.6 fusion.10
  245.1 0.4 fusion.61
  245.5 3.8 convolution_convert_fusion.6
  249.3 0.7 all-gather.9.cloned.1.call-update
  250.0 0.3 all-gather.13.cloned.1.call-start
  250.3 0.6 bitcast_convert_fusion.8
  250.9 0.8 slice_bitcast_fusion
  251.8 31.2 %all-gather.11.cloned.1.call-done = bf16[264,28,128]{2,1,0:T(8,128)(2,1)} async-done(((bf16[33,28,128]{2,1,0:T(8,128)(2,1)}), bf16[264,28,128]{2,1,0:T(8,128)(2,1)}) %all-gather.11.cloned.1.call-update) | async-done | bytes 1892368 | tf_op jit(solution)/shard_map/all_gather | solution.py:148
  283.0 3.6 reshape.379
  286.6 32.0 %all-gather.9.cloned.1.call-done = bf16[1024,1024]{1,0:T(8,128)(2,1)} async-done(((bf16[128,1024]{1,0:T(8,128)(2,1)}), bf16[1024,1024]{1,0:T(8,128)(2,1)}) %all-gather.9.cloned.1.call-update) | async-done | bytes 2097168 | tf_op jit(solution)/shard_map/all_gather | solution.py:61
  318.6 6.6 %convert_reduce_fusion = f32[924,1024]{1,0:T(8,128)S(1)} fusion(bf16[8,924,128]{2,1,0:T(8,128)(2,1)} %reshape.379, bf16[8,128,1024]{2,1,0:T(8,128)(2,1)} %bitcast.129), kind=kOutput, calls=%fused_computation.1 | convolution fusion | flops 1959530496 | bytes 7774208 | tf_op jit(solution)/shard_map/grc,gcn->grn/dot_general | solution.py:24
  325.3 0.9 copy.41
  326.2 1.0 copy-done.5
  327.2 0.2 slice.159
  327.5 3.6 fusion.6
  331.1 5.0 %multiply_convert_fusion = bf16[33,28,8,128]{3,2,1,0:T(8,128)(2,1)S(1)} fusion(f32[8,128]{1,0:T(8,128)S(1)} %bitcast.127, f32[33,28]{1,0:T(8,128)S(1)} %get-tuple-element.22, f32[33,28]{1,0:T(8,128)S(1)} %get-tuple-element.21, f32[33,28,8,128]{3,2,1,0:T(8,128)S(1)} %bitcast.106, bf16[8,33,28,128]{3,2,1,0:T(8,128)(2,1)S(1)} %copy-done.2), kind=kLoop, calls=%fused_computation.15 | loop fusion | flops 5677056 | bytes 7580896 | tf_op jit(solution)/shard_map/convert_element_type | solution.py:14
  336.1 0.1 pad.15
  336.3 0.6 copy.42
  336.8 0.5 copy-done.25
  337.3 0.7 fusion.31
  338.0 0.1 fusion.39
  338.2 0.7 reshape.383
  338.9 1.0 fusion.46
  340.0 1.4 multiply_convert_fusion.1
  341.4 1.1 copy.32
  342.5 0.9 copy.33
  343.4 4.3 %all-to-all-start.1 = ((bf16[8,128,128]{2,1,0:T(8,128)(2,1)}), bf16[8,128,128]{2,1,0:T(8,128)(2,1)}, u32[]{:S(2)}, u32[]{:S(2)}) async-start(bf16[8,128,128]{2,1,0:T(8,128)(2,1)} %bitcast.18), calls=%async_computation.1 | async-start | bytes 524288 | tf_op jit(solution)/shard_map/all_to_all | solution.py:62
  347.9 0.9 copy_convert_fusion
  348.8 0.4 copy-done.7
  349.2 1.9 fusion.7
  351.1 0.2 pad.14
  351.4 2.8 copy.39
  354.1 0.9 convolution_convert_fusion.7
  355.0 19.9 %all-gather.13.cloned.1.call-done = bf16[264,28,128]{2,1,0:T(8,128)(2,1)} async-done(((bf16[33,28,128]{2,1,0:T(8,128)(2,1)}), bf16[264,28,128]{2,1,0:T(8,128)(2,1)}) %all-gather.13.cloned.1.call-update) | async-done | bytes 1892368 | tf_op jit(solution)/shard_map/all_gather | solution.py:169
  374.9 2.5 reshape.384
  377.5 1.6 convert_reduce_fusion.1
  379.1 1.3 fusion.38
  380.4 0.9 select_convert_fusion
  (81 shorter events, 1.2 us)
Async XLA Ops:
  7.2 232.7 %copy-start = (bf16[1024,1,384]{2,0,1:T(8,128)(2,1)S(1)}, bf16[1024,1,384]{2,0,1:T(8,128)(2,1)}, u32[]{:S(2)}) copy-start(bf16[1024,1,384]{2,0,1:T(8,128)(2,1)} %param.24) | copy-start | bytes 2359300
  7.2 1.6 slice-start
  7.2 1.9 slice-start.1
  7.2 1.9 copy-start.11
  7.2 2.0 copy-start.26
  7.2 2.1 copy-start.23
  7.3 2.5 copy-start.24
  22.6 146.9 %all-to-all-start = ((bf16[64,2,11392]{2,1,0:T(2,128)(2,1)}), bf16[64,2,11392]{2,1,0:T(2,128)(2,1)}, u32[]{:S(2)}, u32[]{:S(2)}) async-start(bf16[64,2,11392]{2,1,0:T(2,128)(2,1)} %reshape.407), calls=%async_computation | async-start | bytes 5832704 | tf_op jit(solution)/shard_map/all_to_all | solution.py:90
  42.0 182.9 %all-gather.7.cloned.1.call-start = ((), (), s32[]{:S(2)}) async-start(), calls=%async_computation.2 | async-start | bytes 2433024 | tf_op jit(solution)/shard_map/all_gather | solution.py:119
  186.2 6.2 %copy-start.13 = (s32[33]{0:T(128)S(1)}, s32[33]{0:T(128)}, u32[]{:S(2)}) copy-start(s32[33]{0:T(128)} %param.19) | copy-start | bytes 400
  186.2 6.2 %copy-start.8 = (bf16[33,1,70,256]{3,2,1,0:T(8,128)(2,1)S(1)}, bf16[33,1,70,256]{3,2,1,0:T(8,128)(2,1)}, u32[]{:S(2)}) copy-start(bf16[33,1,70,256]{3,2,1,0:T(8,128)(2,1)} %param.20) | copy-start | bytes 3548164
  189.3 1.6 copy-start.3
  192.1 90.9 %all-gather.11.cloned.1.call-start = ((), (), s32[]{:S(2)}) async-start(), calls=%async_computation.4 | async-start | bytes 2433024 | tf_op jit(solution)/shard_map/all_gather | solution.py:148
  194.7 3.7 copy-start.4
  195.9 34.4 %copy-start.16 = (f32[1024]{0:T(1024)S(1)}, f32[1024]{0:T(1024)}, u32[]{:S(2)}) copy-start(f32[1024]{0:T(1024)} %param.23) | copy-start | bytes 12292
  224.9 5.4 %copy-start.2 = (bf16[8,33,28,128]{3,2,1,0:T(8,128)(2,1)S(1)}, bf16[8,33,28,128]{3,2,1,0:T(8,128)(2,1)}, u32[]{:S(2)}) copy-start(bf16[8,33,28,128]{3,2,1,0:T(8,128)(2,1)} %all-gather.7.cloned.1.call-done) | copy-start | bytes 5677060
  239.9 3.1 copy-start.6
  243.3 1.2 copy-start.9
  245.1 5.2 %copy-start.12 = (bf16[33,8,128]{2,1,0:T(8,128)(2,1)S(1)}, bf16[33,8,128]{2,1,0:T(8,128)(2,1)}, u32[]{:S(2)}) copy-start(bf16[33,8,128]{2,1,0:T(8,128)(2,1)} %param.21) | copy-start | bytes 202756
  245.1 5.2 %copy-start.14 = (bf16[9,128]{1,0:T(8,128)(2,1)S(1)}, bf16[9,128]{1,0:T(8,128)(2,1)}, u32[]{:S(2)}) copy-start(bf16[9,128]{1,0:T(8,128)(2,1)} %param.28) | copy-start | bytes 6916
  249.3 69.4 %all-gather.9.cloned.1.call-start = ((), (), s32[]{:S(2)}) async-start(), calls=%async_computation.3 | async-start | bytes 2359296 | tf_op jit(solution)/shard_map/all_gather | solution.py:61
  250.0 124.9 %all-gather.13.cloned.1.call-start = ((), (), s32[]{:S(2)}) async-start(), calls=%async_computation.5 | async-start | bytes 2433024 | tf_op jit(solution)/shard_map/all_gather | solution.py:169
  325.3 1.9 copy-start.5
  327.4 3.6 copy-start.15
  336.3 1.0 copy-start.25
  338.0 2.0 copy-start.17
  338.0 2.0 copy-start.18
  338.0 2.0 copy-start.19
  338.0 2.0 copy-start.20
  338.0 2.0 copy-start.21
  338.0 2.0 copy-start.22
  343.4 34.0 %all-to-all-start.1 = ((bf16[8,128,128]{2,1,0:T(8,128)(2,1)}), bf16[8,128,128]{2,1,0:T(8,128)(2,1)}, u32[]{:S(2)}, u32[]{:S(2)}) async-start(bf16[8,128,128]{2,1,0:T(8,128)(2,1)} %bitcast.18), calls=%async_computation.1 | async-start | bytes 524288 | tf_op jit(solution)/shard_map/all_to_all | solution.py:62
  347.9 1.3 copy-start.7
  351.3 2.8 copy-start.10
  374.9 6.4 %copy-start.1 = (bf16[1024,1,384]{2,0,1:T(8,128)(2,1)S(1)}, bf16[1024,1,384]{2,0,1:T(8,128)(2,1)}, u32[]{:S(2)}) copy-start(bf16[1024,1,384]{2,0,1:T(8,128)(2,1)} %param.24) | copy-start | bytes 2359300
Sparse Core Ops, SparseCore 0:
  192.2 32.6 all-gather.6
  249.4 33.5 all-gather.10
  285.2 33.4 all-gather.8
  341.5 33.3 all-gather.12
where the time goes:
time: 389 us; the launch traced here: 388 us
  waiting for transfers between devices  238 us (61%)
  local copies, waits for them, and re-layouts  54.9 us (14%)
  other arithmetic  34 us (9%)
  starting transfers between devices  24.2 us (6%)
  matrix products  22.6 us (6%)
  between operations  14.4 us (4%)
    all_to_all x1, waiting for transfers between devices, shards(): lax.all_to_all(jnp.concatenate([frame_send, cache_send], axis=1), 'owner'...  127 us
    unnamed x70, local copies, waits for them, and re-layouts  36.2 us
    all_gather x1, waiting for transfers between devices, shards(): w_out_full = lax.all_gather(w_out, 'ingest', axis=0, tiled=True)  32 us
    all_gather x1, waiting for transfers between devices, shards(): ctx_all = lax.all_gather(context, 'ingest', axis=0, tiled=False)  31.2 us
    all_gather x1, waiting for transfers between devices, shards(): x_all = lax.all_gather(arranged, 'ingest', axis=0, tiled=False)  26.5 us
    all_gather x1, waiting for transfers between devices, shards(): act_all = lax.all_gather(activated, 'ingest', axis=0, tiled=False)  19.9 us
    all_to_all x1, starting transfers between devices, shards(): lax.all_to_all(jnp.concatenate([frame_send, cache_send], axis=1), 'owner'...  19.3 us
    convert_element_type x2, other arithmetic, normalize(): ((values - row_mean) * lax.rsqrt(spread + norm_eps) * gain_cols).astype(j...  10.5 us
  transfers between devices with their start and end apart: 6, of which 5 were waited for; matrix products, arithmetic and copies ran while one was open for 6% of the time, Pallas kernels for 0%

commit v1 on v0

--- a/solution.py
+++ b/solution.py
@@ -5,6 +5,24 @@
 
 BLOCKS = 2
 norm_eps = 1e-05
+
+
+def ring_gather(value, axis, dim):
+    ways, here, step = (lax.axis_size(axis), lax.axis_index(axis), value.shape[dim])
+    dims = [n * ways if d == dim else n for d, n in enumerate(value.shape)]
+    full = lax.dynamic_update_slice_in_dim(
+        jnp.zeros(dims, value.dtype), value, here * step, axis=dim
+    )
+    going_up = going_down = value
+    for far in range(1, ways // 2 + 1):
+        going_up = lax.ppermute(going_up, axis, [(d, (d + 1) % ways) for d in range(ways)])
+        full = lax.dynamic_update_slice_in_dim(full, going_up, (here - far) % ways * step, axis=dim)
+        if 2 * far < ways:
+            going_down = lax.ppermute(going_down, axis, [(d, (d - 1) % ways) for d in range(ways)])
+            full = lax.dynamic_update_slice_in_dim(
+                full, going_down, (here + far) % ways * step, axis=dim
+            )
+    return full
 
 
 def normalize(values, gain_cols):
@@ -58,7 +76,7 @@
     moving = mig_owner.shape[0]
     settled = utterances - moving
     lanes = 128
-    w_out_full = lax.all_gather(w_out, "ingest", axis=0, tiled=True)
+    w_out_full = ring_gather(w_out, "ingest", 0)
     w_pw2_cols = lax.all_to_all(
         w_pw2.reshape(local_width, groups, local_width).transpose(1, 0, 2),
         "ingest",

time: 389 us -> 359 us (0.923)
  waiting for transfers between devices: 238 us -> 189 us
  local copies, waits for them, and re-layouts: 54.9 us -> 64.9 us
  starting transfers between devices: 24.2 us -> 32 us
    all_gather x1 -> x0, waiting for transfers between devices: 32 us -> none  [shards(): w_out_full = lax.all_gather(w_out, 'ingest', axis=0, tiled=True)]
    all_gather x1, waiting for transfers between devices: 31.2 us -> 8.61 us  [shards(): ctx_all = lax.all_gather(context, 'ingest', axis=0, tiled=False)]
    ppermute x0 -> x7, starting transfers between devices: none -> 8.1 us  [the longest x4 4.25 us: ring_gather(): lax.ppermute(going_up, axis, [(d, (d + 1) % ways) for d in range(ways)])]
    dynamic_update_slice x0 -> x8, local copies, waits for them, and re-layouts: none -> 7.71 us  [the longest x4 3.82 us: ring_gather(): lax.dynamic_update_slice_in_dim(full, going_up, (here - far) % ways * ste...]
    ppermute x0 -> x7, waiting for transfers between devices: none -> 7.27 us  [the longest x4 7.26 us: ring_gather(): lax.ppermute(going_up, axis, [(d, (d + 1) % ways) for d in range(ways)])]
    unnamed x70 -> x72, local copies, waits for them, and re-layouts: 36.2 us -> 36.1 us
  transfers between devices with their start and end apart: 6 -> 12, of which waited for: 5 -> 6; matrix products, arithmetic and copies ran while one was open for 6% -> 8% of each run, Pallas kernels for 0% -> 0%
where the time goes in v1:
time: 359 us; the launch traced here: 357 us
  waiting for transfers between devices  189 us (53%)
  local copies, waits for them, and re-layouts  64.9 us (18%)
  other arithmetic  34 us (9%)
  starting transfers between devices  32 us (9%)
  matrix products  22.6 us (6%)
  between operations  14.3 us (4%)
    all_to_all x1, waiting for transfers between devices, shards(): lax.all_to_all(jnp.concatenate([frame_send, cache_send], axis=1), 'owner'...  127 us
    unnamed x72, local copies, waits for them, and re-layouts  36.1 us
    all_gather x1, waiting for transfers between devices, shards(): x_all = lax.all_gather(arranged, 'ingest', axis=0, tiled=False)  26.5 us
    all_gather x1, waiting for transfers between devices, shards(): act_all = lax.all_gather(activated, 'ingest', axis=0, tiled=False)  19.5 us
    all_to_all x1, starting transfers between devices, shards(): lax.all_to_all(jnp.concatenate([frame_send, cache_send], axis=1), 'owner'...  19.3 us
    convert_element_type x2, other arithmetic, normalize(): ((values - row_mean) * lax.rsqrt(spread + norm_eps) * gain_cols).astype(j...  10.5 us
    reduce_sum x2, other arithmetic, normalize(): row_mean = jnp.sum(values, axis=-1, keepdims=True) / model_width  8.92 us
    all_gather x1, waiting for transfers between devices, shards(): ctx_all = lax.all_gather(context, 'ingest', axis=0, tiled=False)  8.61 us
  transfers between devices with their start and end apart: 12, of which 6 were waited for; matrix products, arithmetic and copies ran while one was open for 8% of the time, Pallas kernels for 0%

profile of v1, /device:TPU:1, one launch (start us, length us, event | category | flops | bytes accessed | tf_op | source)
XLA Modules:
  0.0 357.2 jit_solution(10079481334621019486)
XLA Ops:
  7.3 1.5 slice-done
  9.7 0.8 convolution_convert_fusion
  10.5 1.8 maximum_bitcast_fusion
  12.8 5.4 %reduce.8 = bf16[64,22784]{1,0:T(8,128)(2,1)} reduce(bf16[64,1,22784]{2,0,1:T(8,128)(2,1)} %maximum_bitcast_fusion, bf16[]{:T(256)} %broadcast.261), dimensions={1}, to_apply=%copy.30.reduce_sub_computation | reduce | bytes 5832706 | tf_op jit(solution)/shard_map/all_to_all | solution.py:108
  18.2 4.4 %reshape.407 = bf16[64,2,11392]{2,1,0:T(2,128)(2,1)} reshape(bf16[64,22784]{1,0:T(8,128)(2,1)} %reduce.8) | data formatting | bytes 5832704
  22.6 19.3 %all-to-all-start = ((bf16[64,2,11392]{2,1,0:T(2,128)(2,1)}), bf16[64,2,11392]{2,1,0:T(2,128)(2,1)}, u32[]{:S(2)}, u32[]{:S(2)}) async-start(bf16[64,2,11392]{2,1,0:T(2,128)(2,1)} %reshape.407), calls=%async_computation | async-start | bytes 5832704 | tf_op jit(solution)/shard_map/all_to_all | solution.py:108
  42.0 127.4 %all-to-all-done = bf16[64,2,11392]{2,1,0:T(2,128)(2,1)} async-done(((bf16[64,2,11392]{2,1,0:T(2,128)(2,1)}), bf16[64,2,11392]{2,1,0:T(2,128)(2,1)}, u32[]{:S(2)}, u32[]{:S(2)}) %all-to-all-start) | async-done | bytes 2916384 | tf_op jit(solution)/shard_map/all_to_all | solution.py:108
  169.5 16.8 %reshape.408 = bf16[64,1,22784]{2,1,0:T(2,128)(2,1)} reshape(bf16[64,2,11392]{2,1,0:T(2,128)(2,1)} %all-to-all-done) | data formatting | bytes 5832704
  186.2 3.1 copy.57
  189.4 1.4 copy-done.3
  191.2 0.9 all_gather_reshape.3
  192.5 2.2 convolution_convert_fusion.1
  194.7 1.2 slice.143
  195.9 2.5 reshape.378
  198.4 26.5 %all-gather.6.cloned.1.call-done = bf16[8,33,28,128]{3,2,1,0:T(8,128)(2,1)} async-done(((bf16[1,33,28,128]{3,2,1,0:T(8,128)(2,1)}), bf16[8,33,28,128]{3,2,1,0:T(8,128)(2,1)}) %all-gather.6.cloned.1.call-update) | async-done | bytes 1892368 | tf_op jit(solution)/shard_map/all_gather | solution.py:137
  224.9 5.3 %bitcast_reduce_fusion = (f32[33,28]{1,0:T(8,128)S(1)}, f32[33,28]{1,0:T(8,128)S(1)}) fusion(bf16[8,33,28,128]{3,2,1,0:T(8,128)(2,1)} %all-gather.6.cloned.1.call-done), kind=kLoop, calls=%fused_computation.9 | loop fusion | flops 3782856 | bytes 1899744 | tf_op jit(solution)/shard_map/reduce_sum | solution.py:30
  230.2 5.5 %fusion.3 = bf16[33,28,8,128]{3,2,1,0:T(8,128)(2,1)} fusion(f32[8,128]{1,0:T(8,128)S(1)} %bitcast.128, f32[33,28]{1,0:T(8,128)S(1)} %get-tuple-element.24, f32[33,28]{1,0:T(8,128)S(1)} %get-tuple-element.23, bf16[8,33,28,128]{3,2,1,0:T(8,128)(2,1)S(1)} %copy-done.2), kind=kLoop, calls=%fused_computation.13 | loop fusion | flops 4730880 | bytes 3796192 | tf_op jit(solution)/shard_map/convert_element_type | solution.py:32
  235.7 4.1 %convert_element_type.219 = bf16[33,28,1024]{2,1,0:T(8,128)(2,1)} reshape(bf16[33,28,8,128]{3,2,1,0:T(8,128)(2,1)} %fusion.3) | data formatting | bytes 3784704 | tf_op jit(solution)/shard_map/convert_element_type | solution.py:32
  239.8 3.0 convolution_convert_fusion.5
  243.2 1.2 copy-done.9
  244.5 0.6 fusion.10
  245.4 3.8 %convolution_convert_fusion.6 = bf16[33,28,128]{2,1,0:T(8,128)(2,1)} fusion(bf16[33,98,256]{2,1,0:T(8,128)(2,1)} %copy-done.9, f32[33,28]{1,0:T(8,128)S(1)} %fusion.61, f32[33,28,98]{2,1,0:T(8,128)S(1)} %fusion.10), kind=kOutput, calls=%fused_computation.35 | convolution fusion | flops 23572260 | bytes 2216960 | tf_op jit(solution)/shard_map/sqk,skd->sqd/dot_general | solution.py:163
  249.8 3.4 collective-permute-done
  253.2 2.4 collective-permute-start.2
  255.6 0.6 bitcast_convert_fusion.8
  256.2 1.2 collective-permute-start.3
  257.4 1.6 broadcast_in_dim.21
  258.9 0.7 constant_dynamic-update-slice_fusion.7
  259.7 0.7 slice.116
  260.3 1.1 collective-permute-start.4
  261.5 0.7 constant_dynamic-update-slice_fusion.6
  262.2 0.7 constant_dynamic-update-slice_fusion.5
  262.9 2.4 collective-permute-start.5
  265.3 1.7 constant_dynamic-update-slice_fusion.4
  267.5 1.7 constant_dynamic-update-slice_fusion.3
  269.2 0.7 constant_dynamic-update-slice_fusion.2
  269.9 0.7 constant_dynamic-update-slice_fusion.1
  270.6 3.9 %collective-permute-done.6 = bf16[128,1024]{1,0:T(8,128)(2,1)S(1)} collective-permute-done((bf16[128,1024]{1,0:T(8,128)(2,1)S(1)}, bf16[128,1024]{1,0:T(8,128)(2,1)S(1)}, u32[]{:S(2)}, u32[]{:S(2)}) %collective-permute-start.6) | collective-permute-done | bytes 262176 | tf_op jit(solution)/shard_map/ppermute | solution.py:18
  274.5 0.7 constant_dynamic-update-slice_fusion
  275.2 0.8 slice_bitcast_fusion
  276.1 8.6 %all-gather.8.cloned.1.call-done = bf16[264,28,128]{2,1,0:T(8,128)(2,1)} async-done(((bf16[33,28,128]{2,1,0:T(8,128)(2,1)}), bf16[264,28,128]{2,1,0:T(8,128)(2,1)}) %all-gather.8.cloned.1.call-update) | async-done | bytes 1892368 | tf_op jit(solution)/shard_map/all_gather | solution.py:166
  284.7 3.7 %reshape.379 = bf16[8,924,128]{2,1,0:T(8,128)(2,1)} reshape(bf16[264,28,128]{2,1,0:T(8,128)(2,1)} %all-gather.8.cloned.1.call-done) | data formatting | bytes 3784704 | tf_op jit(solution)/shard_map/reshape | solution.py:169
  288.3 6.6 %convert_reduce_fusion = f32[924,1024]{1,0:T(8,128)S(1)} fusion(bf16[8,924,128]{2,1,0:T(8,128)(2,1)} %reshape.379, bf16[8,128,1024]{2,1,0:T(8,128)(2,1)} %bitcast.6), kind=kOutput, calls=%fused_computation.1 | convolution fusion | flops 1959530496 | bytes 7774208 | tf_op jit(solution)/shard_map/grc,gcn->grn/dot_general | solution.py:42
  295.0 0.9 copy.41
  295.9 1.0 copy-done.5
  297.1 3.6 %fusion.6 = (f32[33,28]{1,0:T(8,128)S(1)}, f32[33,28]{1,0:T(8,128)S(1)}) fusion(f32[33,28,8,128]{3,2,1,0:T(8,128)S(1)} %bitcast.105, bf16[8,33,28,128]{3,2,1,0:T(8,128)(2,1)S(1)} %copy-done.2), kind=kLoop, calls=%fused_computation.22 | loop fusion | flops 4729032 | bytes 5684448 | tf_op jit(solution)/shard_map/reduce_sum | solution.py:30
  300.8 5.0 %multiply_convert_fusion = bf16[33,28,8,128]{3,2,1,0:T(8,128)(2,1)S(1)} fusion(f32[8,128]{1,0:T(8,128)S(1)} %bitcast.127, f32[33,28]{1,0:T(8,128)S(1)} %get-tuple-element.22, f32[33,28]{1,0:T(8,128)S(1)} %get-tuple-element.21, f32[33,28,8,128]{3,2,1,0:T(8,128)S(1)} %bitcast.106, bf16[8,33,28,128]{3,2,1,0:T(8,128)(2,1)S(1)} %copy-done.2), kind=kLoop, calls=%fused_computation.15 | loop fusion | flops 5677056 | bytes 7580896 | tf_op jit(solution)/shard_map/convert_element_type | solution.py:32
  306.0 0.6 copy.42
  307.0 0.7 fusion.31
  307.9 0.7 reshape.383
  308.6 1.0 fusion.46
  309.7 1.4 multiply_convert_fusion.1
  311.1 1.1 copy.32
  312.3 0.9 copy.33
  313.1 4.3 %all-to-all-start.1 = ((bf16[8,128,128]{2,1,0:T(8,128)(2,1)}), bf16[8,128,128]{2,1,0:T(8,128)(2,1)}, u32[]{:S(2)}, u32[]{:S(2)}) async-start(bf16[8,128,128]{2,1,0:T(8,128)(2,1)} %bitcast.18), calls=%async_computation.1 | async-start | bytes 524288 | tf_op jit(solution)/shard_map/all_to_all | solution.py:80
  317.6 0.9 copy_convert_fusion
  318.9 1.9 fusion.7
  321.1 2.7 copy.39
  323.8 0.9 convolution_convert_fusion.7
  324.7 19.5 %all-gather.10.cloned.1.call-done = bf16[264,28,128]{2,1,0:T(8,128)(2,1)} async-done(((bf16[33,28,128]{2,1,0:T(8,128)(2,1)}), bf16[264,28,128]{2,1,0:T(8,128)(2,1)}) %all-gather.10.cloned.1.call-update) | async-done | bytes 1892368 | tf_op jit(solution)/shard_map/all_gather | solution.py:187
  344.2 2.5 reshape.384
  346.8 1.6 convert_reduce_fusion.1
  348.4 1.3 fusion.38
  349.7 0.9 select_convert_fusion
  (103 shorter events, 6.1 us)
Async XLA Ops:
  7.2 232.7 %copy-start = (bf16[1024,1,384]{2,0,1:T(8,128)(2,1)S(1)}, bf16[1024,1,384]{2,0,1:T(8,128)(2,1)}, u32[]{:S(2)}) copy-start(bf16[1024,1,384]{2,0,1:T(8,128)(2,1)} %param.24) | copy-start | bytes 2359300
  7.2 1.6 slice-start
  7.2 1.8 slice-start.1
  7.2 1.8 copy-start.11
  7.2 2.0 copy-start.27
  7.2 2.1 copy-start.24
  8.8 0.9 copy-start.25
  22.6 146.9 %all-to-all-start = ((bf16[64,2,11392]{2,1,0:T(2,128)(2,1)}), bf16[64,2,11392]{2,1,0:T(2,128)(2,1)}, u32[]{:S(2)}, u32[]{:S(2)}) async-start(bf16[64,2,11392]{2,1,0:T(2,128)(2,1)} %reshape.407), calls=%async_computation | async-start | bytes 5832704 | tf_op jit(solution)/shard_map/all_to_all | solution.py:108
  41.9 182.9 %all-gather.6.cloned.1.call-start = ((), (), s32[]{:S(2)}) async-start(), calls=%async_computation.2 | async-start | bytes 2433024 | tf_op jit(solution)/shard_map/all_gather | solution.py:137
  186.2 6.2 %copy-start.13 = (s32[33]{0:T(128)S(1)}, s32[33]{0:T(128)}, u32[]{:S(2)}) copy-start(s32[33]{0:T(128)} %param.19) | copy-start | bytes 400
  186.2 6.2 %copy-start.8 = (bf16[33,1,70,256]{3,2,1,0:T(8,128)(2,1)S(1)}, bf16[33,1,70,256]{3,2,1,0:T(8,128)(2,1)}, u32[]{:S(2)}) copy-start(bf16[33,1,70,256]{3,2,1,0:T(8,128)(2,1)} %param.20) | copy-start | bytes 3548164
  189.3 1.6 copy-start.3
  192.0 92.6 %all-gather.8.cloned.1.call-start = ((), (), s32[]{:S(2)}) async-start(), calls=%async_computation.3 | async-start | bytes 2433024 | tf_op jit(solution)/shard_map/all_gather | solution.py:166
  194.7 3.7 %copy-start.4 = (bf16[32,18944]{1,0:T(8,128)(2,1)}, bf16[32,18944]{1,0:T(8,128)(2,1)S(1)}, u32[]{:S(2)}) copy-start(bf16[32,18944]{1,0:T(8,128)(2,1)S(1)} %convolution_convert_fusion.1) | copy-start | bytes 3637252
  195.9 34.4 %copy-start.16 = (f32[1024]{0:T(1024)S(1)}, f32[1024]{0:T(1024)}, u32[]{:S(2)}) copy-start(f32[1024]{0:T(1024)} %param.23) | copy-start | bytes 12292
  224.9 5.4 %copy-start.2 = (bf16[8,33,28,128]{3,2,1,0:T(8,128)(2,1)S(1)}, bf16[8,33,28,128]{3,2,1,0:T(8,128)(2,1)}, u32[]{:S(2)}) copy-start(bf16[8,33,28,128]{3,2,1,0:T(8,128)(2,1)} %all-gather.6.cloned.1.call-done) | copy-start | bytes 5677060
  239.8 3.1 copy-start.6
  243.2 1.2 copy-start.9
  245.0 10.5 %copy-start.14 = (bf16[9,128]{1,0:T(8,128)(2,1)S(1)}, bf16[9,128]{1,0:T(8,128)(2,1)}, u32[]{:S(2)}) copy-start(bf16[9,128]{1,0:T(8,128)(2,1)} %param.28) | copy-start | bytes 6916
  249.2 9.7 %copy-start.12 = (bf16[128,1024]{1,0:T(8,128)(2,1)S(1)}, bf16[128,1024]{1,0:T(8,128)(2,1)}, u32[]{:S(2)}) copy-start(bf16[128,1024]{1,0:T(8,128)(2,1)} %param.25) | copy-start | bytes 786436
  249.2 95.0 %all-gather.10.cloned.1.call-start = ((), (), s32[]{:S(2)}) async-start(), calls=%async_computation.4 | async-start | bytes 2433024 | tf_op jit(solution)/shard_map/all_gather | solution.py:187
  249.3 3.9 %collective-permute-start = (bf16[128,1024]{1,0:T(8,128)(2,1)}, bf16[128,1024]{1,0:T(8,128)(2,1)S(1)}, u32[]{:S(2)}, u32[]{:S(2)}) collective-permute-start(bf16[128,1024]{1,0:T(8,128)(2,1)} %param.25), channel_id=1, source_target_pairs={{0,64},{64,128},{128,192},{192,256},{256,320},{320,384},{384,448},... | collective-permute-start | bytes 786440 | tf_op jit(solution)/shard_map/ppermute | solution.py:18
  249.5 6.6 %collective-permute-start.1 = (bf16[128,1024]{1,0:T(8,128)(2,1)}, bf16[128,1024]{1,0:T(8,128)(2,1)S(1)}, u32[]{:S(2)}, u32[]{:S(2)}) collective-permute-start(bf16[128,1024]{1,0:T(8,128)(2,1)} %param.25), channel_id=1, source_target_pairs={{0,448},{64,0},{128,64},{192,128},{256,192},{320,256},{384,320},{4... | collective-permute-start | bytes 786440 | tf_op jit(solution)/shard_map/ppermute | solution.py:21
  253.2 7.2 %collective-permute-start.2 = (bf16[128,1024]{1,0:T(8,128)(2,1)S(1)}, bf16[128,1024]{1,0:T(8,128)(2,1)}, u32[]{:S(2)}, u32[]{:S(2)}) collective-permute-start(bf16[128,1024]{1,0:T(8,128)(2,1)S(1)} %collective-permute-done), channel_id=1, source_target_pairs={{0,64},{64,128},{128,192},{192,256},{256,320},{320,384},{384,448},... | collective-permute-start | bytes 786440 | tf_op jit(solution)/shard_map/ppermute | solution.py:18
  256.2 6.7 %collective-permute-start.3 = (bf16[128,1024]{1,0:T(8,128)(2,1)S(1)}, bf16[128,1024]{1,0:T(8,128)(2,1)}, u32[]{:S(2)}, u32[]{:S(2)}) collective-permute-start(bf16[128,1024]{1,0:T(8,128)(2,1)S(1)} %collective-permute-done.1), channel_id=1, source_target_pairs={{0,448},{64,0},{128,64},{192,128},{256,192},{320,256},{384,320},{4... | collective-permute-start | bytes 786440 | tf_op jit(solution)/shard_map/ppermute | solution.py:21
  260.3 6.7 %collective-permute-start.4 = (bf16[128,1024]{1,0:T(8,128)(2,1)}, bf16[128,1024]{1,0:T(8,128)(2,1)S(1)}, u32[]{:S(2)}, u32[]{:S(2)}) collective-permute-start(bf16[128,1024]{1,0:T(8,128)(2,1)} %collective-permute-done.2), channel_id=1, source_target_pairs={{0,64},{64,128},{128,192},{192,256},{256,320},{320,384},{384,448},... | collective-permute-start | bytes 786440 | tf_op jit(solution)/shard_map/ppermute | solution.py:18
  262.9 7.0 %collective-permute-start.5 = (bf16[128,1024]{1,0:T(8,128)(2,1)}, bf16[128,1024]{1,0:T(8,128)(2,1)S(1)}, u32[]{:S(2)}, u32[]{:S(2)}) collective-permute-start(bf16[128,1024]{1,0:T(8,128)(2,1)} %collective-permute-done.3), channel_id=1, source_target_pairs={{0,448},{64,0},{128,64},{192,128},{256,192},{320,256},{384,320},{4... | collective-permute-start | bytes 786440 | tf_op jit(solution)/shard_map/ppermute | solution.py:21
  267.0 7.5 %collective-permute-start.6 = (bf16[128,1024]{1,0:T(8,128)(2,1)S(1)}, bf16[128,1024]{1,0:T(8,128)(2,1)S(1)}, u32[]{:S(2)}, u32[]{:S(2)}) collective-permute-start(bf16[128,1024]{1,0:T(8,128)(2,1)S(1)} %collective-permute-done.4), channel_id=1, source_target_pairs={{0,64},{64,128},{128,192},{192,256},{256,320},{320,384},{384,448},... | collective-permute-start | bytes 786440 | tf_op jit(solution)/shard_map/ppermute | solution.py:18
  295.0 1.9 copy-start.5
  297.1 3.6 %copy-start.15 = (f32[1024]{0:T(1024)S(1)}, f32[1024]{0:T(1024)}, u32[]{:S(2)}) copy-start(f32[1024]{0:T(1024)} %param.26) | copy-start | bytes 12292
  305.9 1.0 copy-start.26
  307.7 2.0 copy-start.17
  307.7 2.0 copy-start.18
  307.7 2.0 copy-start.19
  307.7 2.0 copy-start.20
  307.7 2.0 copy-start.21
  307.7 2.0 copy-start.22
  307.7 2.0 copy-start.23
  313.1 33.6 %all-to-all-start.1 = ((bf16[8,128,128]{2,1,0:T(8,128)(2,1)}), bf16[8,128,128]{2,1,0:T(8,128)(2,1)}, u32[]{:S(2)}, u32[]{:S(2)}) async-start(bf16[8,128,128]{2,1,0:T(8,128)(2,1)} %bitcast.18), calls=%async_computation.1 | async-start | bytes 524288 | tf_op jit(solution)/shard_map/all_to_all | solution.py:80
  317.6 1.3 copy-start.7
  321.1 2.8 copy-start.10
  344.2 6.4 %copy-start.1 = (bf16[1024,1,384]{2,0,1:T(8,128)(2,1)S(1)}, bf16[1024,1,384]{2,0,1:T(8,128)(2,1)}, u32[]{:S(2)}) copy-start(bf16[1024,1,384]{2,0,1:T(8,128)(2,1)} %param.24) | copy-start | bytes 2359300
Sparse Core Ops, SparseCore 0:
  192.2 32.6 all-gather.5
  249.3 35.2 all-gather.7
  311.3 32.8 all-gather.9
